TPU v7x, 32 devices: a whole 2x2x4 slice. The times are simulated.
32 devices in a mesh: group: 2 (over y), seq: 4 (over z), batch: 2 (over x), mp: 2 (over core).
Axes of the slice: x: 2, y: 2, z: 4, core: 2. Of those that a mesh axis runs over, the one named last changes fastest.
Arguments:
- features: bfloat16 [4, 512, 384], P(('group', 'batch'), 'seq'), parts along dimension 0, may hold values from -6 to 6
- noise: float32 [4, 512, 384], P(('group', 'batch'), 'seq'), parts along dimension 0, may hold values from -3 to 3
- conv_weight: bfloat16 [5, 384, 768], P(None, 'seq', 'mp'), may hold values from -0.125 to 0.125
- conv_bias: float32 [768], P('mp'), may hold values from -3 to 3
- norm_gain: float32 [768], replicated, may hold values from 0.25 to 1.75
- qkv_weight: bfloat16 [3, 768, 768], P(None, 'seq', 'mp'), may hold values from -1.010363 to 1.010363
- out_weight: bfloat16 [768, 768], P('mp', 'seq'), may hold values from -0.21875 to 0.21875
Outputs:
- block_out: bfloat16 [4, 256, 768], P(('group', 'batch'), 'seq', 'mp'), parts along dimension 0
- new_noise: float32 [4, 512, 384], P(('group', 'batch'), 'seq'), parts along dimension 0
There are 2 independent parts, one for each index of `group`. A program takes and returns all parts, laid end to end along the dimension named above; an argument that names none is the same for every part. Nothing has to cross between parts.
All inputs are finite; a program needn't handle non-finite values.
Results may differ from a plain program's by a relative error of at most 0.014.
Values may be sent and summed in bfloat16 or wider, within the bound.
No kernel may reach another device: no remote copies, remote signals or barrier semaphores. Data moves between devices by JAX's collectives and lax.ppermute only.
A program may use at most 64 MiB of HBM per device.

v0:
```python
import jax
import jax.numpy as jnp
from jax import lax
from jax.sharding import PartitionSpec as P

F = 768
HD = 96
KW = 5
step_size = 0.5
epsilon = 1e-06


def with_halo(cells, sides, width):
    for axis, dim in sides:
        count = lax.axis_size(axis)
        ends = count - 1
        head = lax.slice_in_dim(cells, 0, width, axis=dim)
        tail = lax.slice_in_dim(cells, cells.shape[dim] - width, cells.shape[dim], axis=dim)
        cells = jnp.concatenate(
            [
                lax.ppermute(tail, axis, [(i, (i + 1) % count) for i in range(ends)]),
                cells,
                lax.ppermute(head, axis, [((i + 1) % count, i) for i in range(ends)]),
            ],
            axis=dim,
        )
    return cells


def attend_rows(query, keys, values):
    key_total = keys.shape[0]
    block_len = min(512, key_total)
    head_size = keys.shape[1]
    score_scale = head_size ** (-0.5)
    key_blocks = keys.reshape(key_total // block_len, block_len, head_size)
    value_blocks = values.reshape(key_total // block_len, block_len, head_size)
    query_count = query.shape[0]

    def find_top(carry, key_block):
        row_top, row_mass = carry
        scores = jnp.dot(query, key_block.T, preferred_element_type=jnp.float32) * score_scale
        new_top = jnp.maximum(row_top, jnp.max(scores, axis=1))
        row_mass = row_mass * jnp.exp(row_top - new_top) + jnp.sum(
            jnp.exp(scores - new_top[:, None]), axis=1
        )
        return ((new_top, row_mass), None)

    start_top = jnp.full((query_count,), -1e30, jnp.float32)
    (row_top, row_mass), _ = lax.scan(
        find_top, (start_top, jnp.zeros((query_count,), jnp.float32)), key_blocks
    )
    log_mass = row_top + jnp.log(row_mass)

    def collect(running, blocks):
        key_block, value_block = blocks
        scores = jnp.dot(query, key_block.T, preferred_element_type=jnp.float32) * score_scale
        soft_weights = jnp.exp(scores - log_mass[:, None]).astype(jnp.bfloat16)
        return (
            running + jnp.dot(soft_weights, value_block, preferred_element_type=jnp.float32),
            None,
        )

    running, _ = lax.scan(
        collect, jnp.zeros((query_count, head_size), jnp.float32), (key_blocks, value_blocks)
    )
    return (running.astype(jnp.bfloat16), log_mass)


def attend_back(query, keys, values, attended, log_mass, out_grad):
    key_total = keys.shape[0]
    block_len = min(512, key_total)
    head_size = keys.shape[1]
    score_scale = head_size ** (-0.5)
    key_blocks = keys.reshape(key_total // block_len, block_len, head_size)
    value_blocks = values.reshape(key_total // block_len, block_len, head_size)
    row_dot = jnp.sum(out_grad.astype(jnp.float32) * attended.astype(jnp.float32), axis=1)

    def step_back(query_acc, blocks):
        key_block, value_block = blocks
        scores = jnp.dot(query, key_block.T, preferred_element_type=jnp.float32) * score_scale
        exp_weights = jnp.exp(scores - log_mass[:, None])
        value_part = jnp.einsum(
            "qk,qd->kd",
            exp_weights.astype(jnp.bfloat16),
            out_grad,
            preferred_element_type=jnp.float32,
        )
        prob_grad = jnp.dot(out_grad, value_block.T, preferred_element_type=jnp.float32)
        score_grad = (exp_weights * (prob_grad - row_dot[:, None])).astype(jnp.bfloat16)
        query_acc = (
            query_acc
            + jnp.dot(score_grad, key_block, preferred_element_type=jnp.float32) * score_scale
        )
        key_part = (
            jnp.einsum("qk,qd->kd", score_grad, query, preferred_element_type=jnp.float32)
            * score_scale
        )
        return (query_acc, jnp.concatenate([key_part, value_part], axis=1))

    query_grad, keyval_parts = lax.scan(
        step_back, jnp.zeros((query.shape[0], head_size), jnp.float32), (key_blocks, value_blocks)
    )
    return (query_grad, keyval_parts.reshape(key_total, 2 * head_size))


def forward(stack, conv_weight, conv_bias, norm_gain, qkv_weight, out_weight):
    pass_count, positions, channels = stack.shape
    reach = KW // 2
    half_width = conv_weight.shape[2]
    padded_input = with_halo(stack, (("seq", 1),), reach)
    running = jnp.zeros((pass_count, positions, half_width), jnp.float32)
    piece = lax.all_gather(conv_weight, "seq", axis=1, tiled=True)
    for offset in range(piece.shape[0]):
        running = running + jnp.einsum(
            "ptc,cf->ptf",
            padded_input[:, offset : offset + positions],
            piece[offset],
            preferred_element_type=jnp.float32,
        )
    pre_act = running + conv_bias
    paired = jax.nn.gelu(pre_act).reshape(pass_count, positions // 2, 2, half_width)
    pooled = (0.5 * (paired[:, :, 0] + paired[:, :, 1])).astype(jnp.bfloat16)
    pooled_wide = lax.optimization_barrier(pooled).astype(jnp.float32)
    whole = lax.all_gather(pooled, "mp", axis=2, tiled=True)
    whole_wide = whole.astype(jnp.float32)
    row_scale = lax.rsqrt(jnp.mean(whole_wide * whole_wide, axis=2, keepdims=True) + epsilon)
    normed = (whole_wide * row_scale * norm_gain).astype(jnp.bfloat16)
    rows = positions // 2
    proj_width = qkv_weight.shape[2]
    projected = jnp.einsum(
        "prf,jfh->jprh",
        normed,
        lax.all_gather(qkv_weight, "seq", axis=1, tiled=True),
        preferred_element_type=jnp.float32,
    ).astype(jnp.bfloat16)
    head_size = HD
    head_count = proj_width // head_size
    devices = lax.axis_size("seq")
    query_groups = devices // head_count
    sub_rows = rows // query_groups
    query_send = (
        projected[0]
        .reshape(pass_count, query_groups, sub_rows, head_count, head_size)
        .transpose(3, 1, 0, 2, 4)
        .reshape(devices, pass_count, sub_rows * head_size)
    )
    keyval = jnp.concatenate(
        [
            projected[1].reshape(pass_count, rows, head_count, head_size),
            projected[2].reshape(pass_count, rows, head_count, head_size),
        ],
        axis=3,
    )
    keyval_flat = keyval.transpose(2, 0, 1, 3).reshape(
        head_count, 1, pass_count, rows * 2 * head_size
    )
    keyval_send = jnp.broadcast_to(
        keyval_flat, (head_count, query_groups, pass_count, rows * 2 * head_size)
    ).reshape(devices, pass_count, rows * 2 * head_size)
    query_in, keyval_in = (
        lax.all_to_all(query_send, "seq", split_axis=0, concat_axis=2, tiled=True),
        lax.all_to_all(keyval_send, "seq", split_axis=0, concat_axis=2, tiled=True),
    )
    query_heads = query_in.reshape(pass_count, devices * sub_rows, head_size)
    keyval_heads = keyval_in.reshape(pass_count, devices * rows, 2 * head_size)
    outputs = []
    masses = []
    for index in range(pass_count):
        out_now, mass_now = attend_rows(
            query_heads[index],
            keyval_heads[index, :, :head_size],
            keyval_heads[index, :, head_size:],
        )
        outputs.append(out_now)
        masses.append(mass_now)
    attended_heads = jnp.stack(outputs)
    log_mass = jnp.stack(masses)
    out_send = attended_heads.reshape(pass_count, devices, sub_rows * head_size).transpose(1, 0, 2)
    out_back = lax.all_to_all(out_send, "seq", split_axis=0, concat_axis=0, tiled=True)
    attended = (
        out_back.reshape(head_count, query_groups, pass_count, sub_rows, head_size)
        .transpose(2, 1, 3, 0, 4)
        .reshape(pass_count, rows, proj_width)
    )
    terms = jnp.einsum(
        "prh,hf->prf",
        attended,
        lax.all_gather(out_weight, "seq", axis=1, tiled=True),
        preferred_element_type=jnp.float32,
    )
    mixed = (
        lax.psum_scatter(terms.astype(jnp.bfloat16), "mp", scatter_dimension=2, tiled=True).astype(
            jnp.float32
        )
        + pooled_wide
    )
    return (
        pre_act,
        pooled_wide,
        whole_wide,
        row_scale,
        query_heads,
        keyval_heads,
        attended_heads,
        log_mass,
        mixed,
    )


def shards(features, noise, conv_weight, conv_bias, norm_gain, qkv_weight, out_weight):
    clean = features[0]
    moved = (clean.astype(jnp.float32) + noise[0]).astype(jnp.bfloat16)
    joint = forward(
        jnp.stack([clean, moved]), conv_weight, conv_bias, norm_gain, qkv_weight, out_weight
    )
    clean_run = [item[0:1] for item in joint]
    moved_run = [item[1:2] for item in joint]
    (
        pre_act,
        pooled_wide,
        whole_wide,
        row_scale,
        query_heads,
        keyval_heads,
        attended_heads,
        log_mass,
        mixed,
    ) = [item[0] for item in moved_run]
    clean_mixed = clean_run[8][0]
    rows, half_width = pooled_wide.shape
    positions = pre_act.shape[0]
    proj_width = qkv_weight.shape[2]
    head_size = HD
    head_count = proj_width // head_size
    devices = lax.axis_size("seq")
    query_groups = devices // head_count
    sub_rows = rows // query_groups
    difference = mixed - clean_mixed
    difference_half = difference.astype(jnp.bfloat16)
    difference_whole = lax.all_gather(difference_half, "mp", axis=1, tiled=True)
    out_grad = jnp.einsum(
        "rf,hf->rh",
        difference_whole,
        lax.all_gather(out_weight, "seq", axis=1, tiled=True),
        preferred_element_type=jnp.float32,
    ).astype(jnp.bfloat16)
    grad_send = (
        out_grad.reshape(query_groups, sub_rows, head_count, head_size)
        .transpose(2, 0, 1, 3)
        .reshape(devices, sub_rows * head_size)
    )
    grad_in = lax.all_to_all(grad_send, "seq", split_axis=0, concat_axis=1, tiled=True)
    grad_heads = grad_in.reshape(devices * sub_rows, head_size)
    query_grad, keyval_grad = attend_back(
        query_heads,
        keyval_heads[:, :head_size],
        keyval_heads[:, head_size:],
        attended_heads,
        log_mass,
        grad_heads,
    )
    query_back, keyval_back = (
        lax.all_to_all(
            query_grad.reshape(devices, sub_rows * head_size).astype(jnp.bfloat16),
            "seq",
            split_axis=0,
            concat_axis=0,
            tiled=True,
        ).astype(jnp.float32),
        lax.all_to_all(
            keyval_grad.reshape(devices, rows * 2 * head_size).astype(jnp.bfloat16),
            "seq",
            split_axis=0,
            concat_axis=0,
            tiled=True,
        ).astype(jnp.float32),
    )
    query_rows = (
        query_back.reshape(head_count, query_groups, sub_rows, head_size)
        .transpose(1, 2, 0, 3)
        .reshape(rows, proj_width)
        .astype(jnp.bfloat16)
    )
    keyval_rows = jnp.sum(keyval_back.reshape(head_count, query_groups, rows, 2, head_size), axis=1)
    key_rows = (
        keyval_rows[:, :, 0].transpose(1, 0, 2).reshape(rows, proj_width).astype(jnp.bfloat16)
    )
    value_rows = (
        keyval_rows[:, :, 1].transpose(1, 0, 2).reshape(rows, proj_width).astype(jnp.bfloat16)
    )
    grads = jnp.stack([query_rows, key_rows, value_rows])
    normed_terms = jnp.einsum(
        "jrh,jfh->rf",
        grads,
        lax.all_gather(qkv_weight, "seq", axis=1, tiled=True),
        preferred_element_type=jnp.float32,
    )
    offset_mp = lax.axis_index("mp") * half_width
    gain_own = lax.dynamic_slice_in_dim(norm_gain, offset_mp, half_width, 0)
    normed_grad = lax.psum_scatter(
        normed_terms.astype(jnp.bfloat16), "mp", scatter_dimension=1, tiled=True
    ).astype(jnp.float32)
    weighted = lax.psum(jnp.sum(normed_grad * gain_own * pooled_wide, axis=1, keepdims=True), "mp")
    pooled_grad = (
        difference + row_scale * gain_own * normed_grad - pooled_wide * row_scale**3 * weighted / F
    )
    spread = jnp.broadcast_to((0.5 * pooled_grad)[:, None, :], (rows, 2, half_width)).reshape(
        positions, half_width
    )
    gelu_back = jax.vjp(jax.nn.gelu, pre_act)[1]
    pre_grad = gelu_back(spread)[0].astype(jnp.bfloat16)
    reach = KW // 2
    padded = with_halo(pre_grad, (("seq", 0),), reach)
    piece = lax.all_gather(conv_weight, "seq", axis=1, tiled=True)
    running = jnp.zeros((positions, piece.shape[1]), jnp.float32)
    for offset in range(piece.shape[0]):
        lower = 2 * reach - offset
        running = running + jnp.einsum(
            "tf,cf->tc",
            padded[lower : lower + positions],
            piece[offset],
            preferred_element_type=jnp.float32,
        )
    input_grad = lax.psum(running.astype(jnp.bfloat16), "mp").astype(jnp.float32)
    new_noise = noise[0] + step_size * input_grad * lax.rsqrt(
        jnp.mean(input_grad * input_grad, axis=1, keepdims=True) + epsilon
    )
    return (clean_mixed.astype(jnp.bfloat16)[None], new_noise[None])


def solution(mesh):
    return jax.shard_map(
        shards,
        mesh=mesh,
        in_specs=(
            P(("group", "batch"), "seq", None),
            P(("group", "batch"), "seq", None),
            P(None, "seq", "mp"),
            P("mp"),
            P(),
            P(None, "seq", "mp"),
            P("mp", "seq"),
        ),
        out_specs=(P(("group", "batch"), "seq", "mp"), P(("group", "batch"), "seq", None)),
        check_vma=False,
    )
```

profile of v0, /device:TPU:0, one launch (start us, length us, event | category | flops | bytes accessed | tf_op | source)
XLA Modules:
  0.0 244.7 jit_solution(5682853137255914638)
XLA Ops:
  7.2 0.7 all-gather.4.cloned.1.call-update
  8.0 0.7 all-gather.6.cloned.1.call-update
  8.7 1.0 add_convert_fusion
  9.7 0.7 pad_maximum_fusion.7
  10.4 4.9 %collective-permute-start = (bf16[2,2,384]{2,1,0:T(2,128)(2,1)S(1)}, bf16[2,2,384]{2,1,0:T(2,128)(2,1)S(1)}, u32[]{:S(2)}, u32[]{:S(2)}) collective-permute-start(bf16[2,2,384]{2,1,0:T(2,128)(2,1)S(1)} %get-tuple-element.88), channel_id=1, source_target_pairs={{0,4},{4,8},{8,12},{1,5},{5,9},{9,13},{2,6},{6,10},{10,14},{3,7},{... | collective-permute-start | bytes 9224 | tf_op jit(solution)/shard_map/ppermute | solution.py:21
  15.4 1.3 collective-permute-start.1
  16.7 4.2 %collective-permute-done.1 = bf16[2,2,384]{2,1,0:T(2,128)(2,1)S(1)} collective-permute-done((bf16[2,2,384]{2,1,0:T(2,128)(2,1)S(1)}, bf16[2,2,384]{2,1,0:T(2,128)(2,1)S(1)}, u32[]{:S(2)}, u32[]{:S(2)}) %collective-permute-start.1) | collective-permute-done | bytes 3104 | tf_op jit(solution)/shard_map/ppermute | solution.py:23
  20.9 26.7 %all-gather.4.cloned.1.call-done = bf16[5,384,384]{2,1,0:T(8,128)(2,1)} async-done(((bf16[5,96,384]{2,1,0:T(8,128)(2,1)}), bf16[5,384,384]{2,1,0:T(8,128)(2,1)}) %all-gather.4.cloned.1.call-update) | async-done | bytes 1474576 | tf_op jit(solution)/shard_map/all_gather | solution.py:112
  47.6 1.3 fusion.38
  49.0 1.2 fusion.42
  51.9 1.9 all-gather
  54.0 34.5 %all-gather.6.cloned.1.call-done = bf16[3,768,384]{2,1,0:T(8,128)(2,1)} async-done(((bf16[3,192,384]{2,1,0:T(8,128)(2,1)}), bf16[3,768,384]{2,1,0:T(8,128)(2,1)}) %all-gather.6.cloned.1.call-update) | async-done | bytes 1769488 | tf_op jit(solution)/shard_map/all_gather | solution.py:133
  88.5 2.0 fusion.8
  90.6 0.9 reshape.242
  91.5 3.3 %all-to-all-start = ((bf16[4,2,6144]{2,1,0:T(2,128)(2,1)}), bf16[4,2,6144]{2,1,0:T(2,128)(2,1)S(1)}, u32[]{:S(2)}, u32[]{:S(2)}) async-start(bf16[4,2,6144]{2,1,0:T(2,128)(2,1)} %reshape.242), calls=%async_computation | async-start | bytes 196608 | tf_op jit(solution)/shard_map/all_to_all | solution.py:161
  95.3 1.0 reshape_reshape.4
  96.3 4.3 %all-to-all-done = bf16[4,2,6144]{2,1,0:T(2,128)(2,1)S(1)} async-done(((bf16[4,2,6144]{2,1,0:T(2,128)(2,1)}), bf16[4,2,6144]{2,1,0:T(2,128)(2,1)S(1)}, u32[]{:S(2)}, u32[]{:S(2)}) %all-to-all-start) | async-done | bytes 98336 | tf_op jit(solution)/shard_map/all_to_all | solution.py:161
  100.6 3.4 %all-to-all-start.1 = ((bf16[4,2,12288]{2,1,0:T(2,128)(2,1)}), bf16[4,2,12288]{2,1,0:T(2,128)(2,1)S(1)}, u32[]{:S(2)}, u32[]{:S(2)}) async-start(bf16[4,2,12288]{2,1,0:T(2,128)(2,1)} %reshape_reshape.4), calls=%async_computation.1 | async-start | bytes 393216 | tf_op jit(solution)/shard_map/all_to_all | solution.py:162
  104.6 5.5 %all-to-all-done.1 = bf16[4,2,12288]{2,1,0:T(2,128)(2,1)S(1)} async-done(((bf16[4,2,12288]{2,1,0:T(2,128)(2,1)}), bf16[4,2,12288]{2,1,0:T(2,128)(2,1)S(1)}, u32[]{:S(2)}, u32[]{:S(2)}) %all-to-all-start.1) | async-done | bytes 196640 | tf_op jit(solution)/shard_map/all_to_all | solution.py:162
  112.5 0.7 copy.103
  113.2 3.3 %all-to-all-start.2 = ((bf16[4,2,6144]{2,1,0:T(2,128)(2,1)}), bf16[4,2,6144]{2,1,0:T(2,128)(2,1)S(1)}, u32[]{:S(2)}, u32[]{:S(2)}) async-start(bf16[4,2,6144]{2,1,0:T(2,128)(2,1)} %copy.103), calls=%async_computation.2 | async-start | bytes 196608 | tf_op jit(solution)/shard_map/all_to_all | solution.py:179
  116.6 16.8 %all_gather.21 = bf16[384,768]{0,1:T(8,128)(2,1)S(1)} all-gather(bf16[384,192]{0,1:T(8,128)(2,1)S(1)} %copy-done.8), channel_id=1, replica_groups=mesh['group'=2,'seq'=4,'batch'=2,'mp'=2] {'seq'}, dimensions={1}, use_global_device_ids=true | all-gather | bytes 737280 | tf_op jit(solution)/shard_map/all_gather | solution.py:188
  134.5 0.9 reshape.261
  135.5 0.7 convert_element_type.202
  136.2 0.8 squeeze.90
  137.8 5.3 %reduce-scatter.7.cloned.1.call-done = bf16[384,128]{1,0:T(8,128)(2,1)} async-done(((bf16[768,128]{1,0:T(8,128)(2,1)}), bf16[384,128]{1,0:T(8,128)(2,1)}) %reduce-scatter.7.cloned.1.call-update) | async-done | bytes 98320
  143.0 1.0 reshape.262
  144.3 1.9 all_gather.22
  147.1 0.9 reduce.9
  148.7 4.8 %all-to-all-start.3 = ((bf16[4,2,3072]{2,1,0:T(2,128)(2,1)}), bf16[4,2,3072]{2,1,0:T(2,128)(2,1)S(1)}, u32[]{:S(2)}, u32[]{:S(2)}) async-start(bf16[4,2,3072]{2,1,0:T(2,128)(2,1)} %reshape.271), calls=%async_computation.3 | async-start | bytes 98304 | tf_op jit(solution)/shard_map/all_to_all | solution.py:252
  153.7 5.5 %all-to-all-done.3 = bf16[4,2,3072]{2,1,0:T(2,128)(2,1)S(1)} async-done(((bf16[4,2,3072]{2,1,0:T(2,128)(2,1)}), bf16[4,2,3072]{2,1,0:T(2,128)(2,1)S(1)}, u32[]{:S(2)}, u32[]{:S(2)}) %all-to-all-start.3) | async-done | bytes 49184 | tf_op jit(solution)/shard_map/all_to_all | solution.py:252
  161.0 0.9 reduce.11
  162.6 3.5 %all-to-all-start.4 = ((bf16[4,2,3072]{2,1,0:T(2,128)(2,1)}), bf16[4,2,3072]{2,1,0:T(2,128)(2,1)S(1)}, u32[]{:S(2)}, u32[]{:S(2)}) async-start(bf16[4,2,3072]{2,1,0:T(2,128)(2,1)} %reshape.275), calls=%async_computation.4 | async-start | bytes 98304 | tf_op jit(solution)/shard_map/all_to_all | solution.py:263
  166.3 1.2 reduce.10
  167.6 0.8 reshape.273
  168.3 3.2 %all-to-all-done.4 = bf16[4,2,3072]{2,1,0:T(2,128)(2,1)S(1)} async-done(((bf16[4,2,3072]{2,1,0:T(2,128)(2,1)}), bf16[4,2,3072]{2,1,0:T(2,128)(2,1)S(1)}, u32[]{:S(2)}, u32[]{:S(2)}) %all-to-all-start.4) | async-done | bytes 49184 | tf_op jit(solution)/shard_map/all_to_all | solution.py:263
  172.1 3.9 %all-to-all-start.5 = ((bf16[4,2,6144]{2,1,0:T(2,128)(2,1)}), bf16[4,2,6144]{2,1,0:T(2,128)(2,1)}, u32[]{:S(2)}, u32[]{:S(2)}) async-start(bf16[4,2,6144]{2,1,0:T(2,128)(2,1)} %reshape.273), calls=%async_computation.5 | async-start | bytes 196608 | tf_op jit(solution)/shard_map/all_to_all | solution.py:270
  176.1 1.0 reshape.276
  177.1 0.9 reduce.4
  178.0 0.9 convert_element_type.211
  178.9 0.7 copy.112
  179.6 1.6 convert_element_type.213
  181.1 0.8 all-to-all-done.5
  181.9 1.7 reshape.274
  183.6 1.5 reduce.5
  185.1 0.8 convert_element_type.216
  185.9 1.2 fusion.123
  187.8 0.7 convert_element_type.219
  188.6 0.9 copy.116
  189.5 0.7 convert_element_type.222
  190.2 1.5 fusion.17
  191.7 0.8 copy.129
  192.6 8.3 %reduce-scatter.9.cloned.1.call-done = bf16[384,64]{1,0:T(8,128)(2,1)} async-done(((bf16[768,64]{1,0:T(8,128)(2,1)}), bf16[384,64]{1,0:T(8,128)(2,1)}) %reduce-scatter.9.cloned.1.call-update) | async-done | bytes 49168
  200.9 1.0 copy.130
  201.9 1.0 fusion.106
  202.9 2.5 %psum.14 = f32[64]{0:T(128)S(1)} all-reduce(f32[64]{0:T(128)S(1)} %fusion.106), channel_id=1, replica_groups=mesh['group'=2,'seq'=4,'batch'=2,'mp'=2] {'mp'}, use_global_device_ids=true, to_apply=%region_9.0 | all-reduce | flops 64 | bytes 512 | tf_op jit(solution)/shard_map/psum | solution.py:303
  205.4 1.0 broadcast_multiply_fusion
  206.8 1.3 collective-permute-start.2
  208.4 4.5 %collective-permute-start.3 = (bf16[2,384]{1,0:T(2,128)(2,1)S(1)}, bf16[2,384]{1,0:T(2,128)(2,1)S(1)}, u32[]{:S(2)}, u32[]{:S(2)}) collective-permute-start(bf16[2,384]{1,0:T(2,128)(2,1)S(1)} %get-tuple-element.93), channel_id=1, source_target_pairs={{0,4},{4,8},{8,12},{1,5},{5,9},{9,13},{2,6},{6,10},{10,14},{3,7},{... | collective-permute-start | bytes 4616 | tf_op jit(solution)/shard_map/ppermute | solution.py:21
  213.4 0.8 collective-permute-done.3
  214.7 0.9 fusion.18
  216.2 19.2 %all-reduce.2.cloned.1.call-done = bf16[128,384]{1,0:T(8,128)(2,1)} async-done(((bf16[128,384]{1,0:T(8,128)(2,1)}), bf16[128,384]{1,0:T(8,128)(2,1)}) %all-reduce.2.cloned.1.call-update) | async-done | bytes 98320 | tf_op jit(solution)/shard_map/psum | solution.py:324
  235.5 1.0 fusion.58
  236.5 1.7 fusion.60
  (122 shorter events, 15.7 us)
Async XLA Ops:
  7.2 13.7 %copy-start.4 = (bf16[1,128,384]{2,1,0:T(8,128)(2,1)S(1)}, bf16[1,128,384]{2,1,0:T(8,128)(2,1)}, u32[]{:S(2)}) copy-start(bf16[1,128,384]{2,1,0:T(8,128)(2,1)} %param.7) | copy-start | bytes 294916
  7.2 40.5 %all-gather.4.cloned.1.call-start = ((), (), s32[]{:S(2)}) async-start(), calls=%async_computation.8 | async-start | bytes 1843200 | tf_op jit(solution)/shard_map/all_gather | solution.py:112
  7.9 80.5 %all-gather.6.cloned.1.call-start = ((), (), s32[]{:S(2)}) async-start(), calls=%async_computation.9 | async-start | bytes 2211840 | tf_op jit(solution)/shard_map/all_gather | solution.py:133
  10.4 6.3 %collective-permute-start = (bf16[2,2,384]{2,1,0:T(2,128)(2,1)S(1)}, bf16[2,2,384]{2,1,0:T(2,128)(2,1)S(1)}, u32[]{:S(2)}, u32[]{:S(2)}) collective-permute-start(bf16[2,2,384]{2,1,0:T(2,128)(2,1)S(1)} %get-tuple-element.88), channel_id=1, source_target_pairs={{0,4},{4,8},{8,12},{1,5},{5,9},{9,13},{2,6},{6,10},{10,14},{3,7},{... | collective-permute-start | bytes 9224 | tf_op jit(solution)/shard_map/ppermute | solution.py:21
  15.4 5.5 %collective-permute-start.1 = (bf16[2,2,384]{2,1,0:T(2,128)(2,1)S(1)}, bf16[2,2,384]{2,1,0:T(2,128)(2,1)S(1)}, u32[]{:S(2)}, u32[]{:S(2)}) collective-permute-start(bf16[2,2,384]{2,1,0:T(2,128)(2,1)S(1)} %get-tuple-element.89), channel_id=1, source_target_pairs={{4,0},{8,4},{12,8},{5,1},{9,5},{13,9},{6,2},{10,6},{14,10},{7,3},{... | collective-permute-start | bytes 9224 | tf_op jit(solution)/shard_map/ppermute | solution.py:23
  47.6 2.6 %copy-start.1 = (bf16[5,384,384]{2,1,0:T(8,128)(2,1)S(1)}, bf16[5,384,384]{2,1,0:T(8,128)(2,1)}, u32[]{:S(2)}) copy-start(bf16[5,384,384]{2,1,0:T(8,128)(2,1)} %all-gather.4.cloned.1.call-done) | copy-start | bytes 4423684
  50.2 0.7 copy-start.10
  51.3 84.9 %copy-start.2 = (f32[2,128,384]{2,1,0:T(8,128)}, f32[2,128,384]{2,1,0:T(8,128)S(1)}, u32[]{:S(2)}) copy-start(f32[2,128,384]{2,1,0:T(8,128)S(1)} %get-tuple-element.95) | copy-start | bytes 1179652
  51.3 37.1 %copy-start.9 = (f32[768]{0:T(1024)S(1)}, f32[768]{0:T(1024)}, u32[]{:S(2)}) copy-start(f32[768]{0:T(1024)} %param.11) | copy-start | bytes 9220
  91.5 9.1 %all-to-all-start = ((bf16[4,2,6144]{2,1,0:T(2,128)(2,1)}), bf16[4,2,6144]{2,1,0:T(2,128)(2,1)S(1)}, u32[]{:S(2)}, u32[]{:S(2)}) async-start(bf16[4,2,6144]{2,1,0:T(2,128)(2,1)} %reshape.242), calls=%async_computation | async-start | bytes 196608 | tf_op jit(solution)/shard_map/all_to_all | solution.py:161
  100.6 9.6 %all-to-all-start.1 = ((bf16[4,2,12288]{2,1,0:T(2,128)(2,1)}), bf16[4,2,12288]{2,1,0:T(2,128)(2,1)S(1)}, u32[]{:S(2)}, u32[]{:S(2)}) async-start(bf16[4,2,12288]{2,1,0:T(2,128)(2,1)} %reshape_reshape.4), calls=%async_computation.1 | async-start | bytes 393216 | tf_op jit(solution)/shard_map/all_to_all | solution.py:162
  110.6 6.0 %copy-start.8 = (bf16[384,192]{0,1:T(8,128)(2,1)S(1)}, bf16[384,192]{0,1:T(8,128)(2,1)}, u32[]{:S(2)}) copy-start(bf16[384,192]{0,1:T(8,128)(2,1)} %param.13) | copy-start | bytes 442372
  113.2 20.2 %all-to-all-start.2 = ((bf16[4,2,6144]{2,1,0:T(2,128)(2,1)}), bf16[4,2,6144]{2,1,0:T(2,128)(2,1)S(1)}, u32[]{:S(2)}, u32[]{:S(2)}) async-start(bf16[4,2,6144]{2,1,0:T(2,128)(2,1)} %copy.103), calls=%async_computation.2 | async-start | bytes 196608 | tf_op jit(solution)/shard_map/all_to_all | solution.py:179
  116.6 26.5 %reduce-scatter.7.cloned.1.call-start = ((), (), s32[]{:S(2)}) async-start(), calls=%async_computation.11 | async-start | bytes 294912
  148.7 10.5 %all-to-all-start.3 = ((bf16[4,2,3072]{2,1,0:T(2,128)(2,1)}), bf16[4,2,3072]{2,1,0:T(2,128)(2,1)S(1)}, u32[]{:S(2)}, u32[]{:S(2)}) async-start(bf16[4,2,3072]{2,1,0:T(2,128)(2,1)} %reshape.271), calls=%async_computation.3 | async-start | bytes 98304 | tf_op jit(solution)/shard_map/all_to_all | solution.py:252
  162.6 8.9 %all-to-all-start.4 = ((bf16[4,2,3072]{2,1,0:T(2,128)(2,1)}), bf16[4,2,3072]{2,1,0:T(2,128)(2,1)S(1)}, u32[]{:S(2)}, u32[]{:S(2)}) async-start(bf16[4,2,3072]{2,1,0:T(2,128)(2,1)} %reshape.275), calls=%async_computation.4 | async-start | bytes 98304 | tf_op jit(solution)/shard_map/all_to_all | solution.py:263
  171.5 0.6 copy-start.7
  172.1 9.8 %all-to-all-start.5 = ((bf16[4,2,6144]{2,1,0:T(2,128)(2,1)}), bf16[4,2,6144]{2,1,0:T(2,128)(2,1)}, u32[]{:S(2)}, u32[]{:S(2)}) async-start(bf16[4,2,6144]{2,1,0:T(2,128)(2,1)} %reshape.273), calls=%async_computation.5 | async-start | bytes 196608 | tf_op jit(solution)/shard_map/all_to_all | solution.py:270
  176.0 14.2 %copy-start = (bf16[3,768,384]{2,1,0:T(8,128)(2,1)S(1)}, bf16[3,768,384]{2,1,0:T(8,128)(2,1)}, u32[]{:S(2)}) copy-start(bf16[3,768,384]{2,1,0:T(8,128)(2,1)} %all-gather.6.cloned.1.call-done) | copy-start | bytes 5308420
  176.1 24.8 %reduce-scatter.9.cloned.1.call-start = ((), (), s32[]{:S(2)}) async-start(), calls=%async_computation.12 | async-start | bytes 294912
  191.7 14.9 %copy-start.3 = (f32[2,128,384]{2,1,0:T(8,128)S(1)}, f32[2,128,384]{2,1,0:T(8,128)}, u32[]{:S(2)}) copy-start(f32[2,128,384]{2,1,0:T(8,128)} %copy-done.2) | copy-start | bytes 1179652
  191.7 16.4 %copy-start.6 = (f32[64,2,384]{2,1,0:T(2,128)S(1)}, f32[64,2,384]{2,1,0:T(2,128)}, u32[]{:S(2)}) copy-start(f32[64,2,384]{2,1,0:T(2,128)} %squeeze.90) | copy-start | bytes 589828
  192.6 42.9 %all-reduce.2.cloned.1.call-start = ((), (), s32[]{:S(2)}) async-start(), calls=%async_computation.10 | async-start | bytes 196608 | tf_op jit(solution)/shard_map/psum | solution.py:324
  206.8 6.4 %collective-permute-start.2 = (bf16[2,384]{1,0:T(2,128)(2,1)S(1)}, bf16[2,384]{1,0:T(2,128)(2,1)S(1)}, u32[]{:S(2)}, u32[]{:S(2)}) collective-permute-start(bf16[2,384]{1,0:T(2,128)(2,1)S(1)} %get-tuple-element.92), channel_id=1, source_target_pairs={{4,0},{8,4},{12,8},{5,1},{9,5},{13,9},{6,2},{10,6},{14,10},{7,3},{... | collective-permute-start | bytes 4616 | tf_op jit(solution)/shard_map/ppermute | solution.py:23
  208.4 5.8 %collective-permute-start.3 = (bf16[2,384]{1,0:T(2,128)(2,1)S(1)}, bf16[2,384]{1,0:T(2,128)(2,1)S(1)}, u32[]{:S(2)}, u32[]{:S(2)}) collective-permute-start(bf16[2,384]{1,0:T(2,128)(2,1)S(1)} %get-tuple-element.93), channel_id=1, source_target_pairs={{0,4},{4,8},{8,12},{1,5},{5,9},{9,13},{2,6},{6,10},{10,14},{3,7},{... | collective-permute-start | bytes 4616 | tf_op jit(solution)/shard_map/ppermute | solution.py:21
  213.4 23.1 %copy-start.5 = (f32[1,128,384]{2,1,0:T(8,128)S(1)}, f32[1,128,384]{2,1,0:T(8,128)}, u32[]{:S(2)}) copy-start(f32[1,128,384]{2,1,0:T(8,128)} %param.8) | copy-start | bytes 589828
Sparse Core Ops, SparseCore 0:
  9.6 38.0 all-gather.3
  49.2 39.1 all-gather.5
  135.6 7.4 reduce-scatter.6
  192.7 8.1 reduce-scatter.8
  215.7 19.7 all-reduce.1
where the time goes:
time: 246 us; the launch traced here: 245 us
  waiting for transfers between devices  120 us (49%)
  starting transfers between devices  34.4 us (14%)
  local copies, waits for them, and re-layouts  27.7 us (11%)
  blocking collectives  23.1 us (9%)
  between operations  14.6 us (6%)
  other arithmetic  13.9 us (6%)
  matrix products  11.3 us (5%)
    all_gather x1, waiting for transfers between devices, forward(): lax.all_gather(qkv_weight, 'seq', axis=1, tiled=True)  34.5 us
    all_gather x1, waiting for transfers between devices, forward(): piece = lax.all_gather(conv_weight, 'seq', axis=1, tiled=True)  26.7 us
    psum x1, waiting for transfers between devices, shards(): lax.psum(running.astype(jnp.bfloat16), 'mp').astype(jnp.float32)  19.2 us
    all_gather x1, blocking collectives, forward(): lax.all_gather(out_weight, 'seq', axis=1, tiled=True)  16.8 us
    unnamed x7, waiting for transfers between devices  14.9 us
    unnamed x34, local copies, waits for them, and re-layouts  9.74 us
    ppermute x2, starting transfers between devices, with_halo(): lax.ppermute(tail, axis, [(i, (i + 1) % count) for i in range(ends)])  9.49 us
    all_to_all x1, waiting for transfers between devices, forward(): lax.all_to_all(keyval_send, 'seq', split_axis=0, concat_axis=2, tiled=True)  5.54 us
  transfers between devices with their start and end apart: 15, of which 12 were waited for; matrix products, arithmetic and copies ran while one was open for 8% of the time, Pallas kernels for 0%

commit v1 on v0

--- a/solution.py
+++ b/solution.py
@@ -8,6 +8,19 @@
 KW = 5
 step_size = 0.5
 epsilon = 1e-06
+
+
+def collect_2(x, axis, dim):
+    ways = lax.axis_size(axis)
+    up = [(d, (d + 1) % ways) for d in range(ways)]
+    down = [(d, (d - 1) % ways) for d in range(ways)]
+    earlier, later = ([x], [x])
+    for _ in range(ways // 2):
+        earlier.append(lax.ppermute(earlier[-1], axis, up))
+    for _ in range((ways - 1) // 2):
+        later.append(lax.ppermute(later[-1], axis, down))
+    line = jnp.concatenate([*earlier[::-1], *later[1:]], axis=dim)
+    return jnp.roll(line, (lax.axis_index(axis) - ways // 2) * x.shape[dim], axis=dim)
 
 
 def with_halo(cells, sides, width):
@@ -183,10 +196,7 @@
         .reshape(pass_count, rows, proj_width)
     )
     terms = jnp.einsum(
-        "prh,hf->prf",
-        attended,
-        lax.all_gather(out_weight, "seq", axis=1, tiled=True),
-        preferred_element_type=jnp.float32,
+        "prh,hf->prf", attended, collect_2(out_weight, "seq", 1), preferred_element_type=jnp.float32
     )
     mixed = (
         lax.psum_scatter(terms.astype(jnp.bfloat16), "mp", scatter_dimension=2, tiled=True).astype(

time: 246 us -> 258 us (1.049)
  local copies, waits for them, and re-layouts: 27.7 us -> 34.4 us
  starting transfers between devices: 34.4 us -> 37.6 us
    ppermute x0 -> x3, waiting for transfers between devices: none -> 8.86 us  [the longest x2 8.86 us: collect_2(): earlier.append(lax.ppermute(earlier[-1], axis, up))]
    all_to_all x1, waiting for transfers between devices: 5.54 us -> 0.01 us  [forward(): lax.all_to_all(keyval_send, 'seq', split_axis=0, concat_axis=2, tiled=True)]
    unnamed x7, waiting for transfers between devices: 14.9 us -> 9.7 us
    ppermute x0 -> x3, starting transfers between devices: none -> 4.64 us  [the longest x2 2.77 us: collect_2(): earlier.append(lax.ppermute(earlier[-1], axis, up))]
    ppermute x2, waiting for transfers between devices: 4.18 us -> 7.86 us  [with_halo(): lax.ppermute(head, axis, [((i + 1) % count, i) for i in range(ends)])]
    all_to_all x1, waiting for transfers between devices: 0.01 us -> 2.64 us  [forward(): lax.all_to_all(out_send, 'seq', split_axis=0, concat_axis=0, tiled=True)]
    unnamed x34 -> x53, local copies, waits for them, and re-layouts: 9.74 us -> 12 us
  transfers between devices with their start and end apart: 15 -> 18, of which waited for: 12 -> 12; matrix products, arithmetic and copies ran while one was open for 8% -> 10% of each run, Pallas kernels for 0% -> 0%
where the time goes in v1:
time: 258 us; the launch traced here: 257 us
  waiting for transfers between devices  121 us (47%)
  starting transfers between devices  37.6 us (15%)
  local copies, waits for them, and re-layouts  34.4 us (13%)
  blocking collectives  21.6 us (8%)
  between operations  14.7 us (6%)
  other arithmetic  13.9 us (5%)
  matrix products  13.8 us (5%)
    all_gather x1, waiting for transfers between devices, forward(): lax.all_gather(qkv_weight, 'seq', axis=1, tiled=True)  33.8 us
    all_gather x1, waiting for transfers between devices, forward(): piece = lax.all_gather(conv_weight, 'seq', axis=1, tiled=True)  26.7 us
    psum x1, waiting for transfers between devices, shards(): lax.psum(running.astype(jnp.bfloat16), 'mp').astype(jnp.float32)  17.4 us
    all_gather x1, blocking collectives, shards(): lax.all_gather(out_weight, 'seq', axis=1, tiled=True)  15.2 us
    unnamed x53, local copies, waits for them, and re-layouts  12 us
    unnamed x7, waiting for transfers between devices  9.7 us
    ppermute x2, waiting for transfers between devices, collect_2(): earlier.append(lax.ppermute(earlier[-1], axis, up))  8.86 us
    ppermute x2, starting transfers between devices, with_halo(): lax.ppermute(tail, axis, [(i, (i + 1) % count) for i in range(ends)])  8.56 us
  transfers between devices with their start and end apart: 18, of which 12 were waited for; matrix products, arithmetic and copies ran while one was open for 10% of the time, Pallas kernels for 0%

profile of v1, /device:TPU:0, one launch (start us, length us, event | category | flops | bytes accessed | tf_op | source)
XLA Modules:
  0.0 256.6 jit_solution(3474220659920675946)
XLA Ops:
  8.7 1.0 add_convert_fusion
  10.4 4.9 %collective-permute-start = (bf16[2,2,384]{2,1,0:T(2,128)(2,1)S(1)}, bf16[2,2,384]{2,1,0:T(2,128)(2,1)S(1)}, u32[]{:S(2)}, u32[]{:S(2)}) collective-permute-start(bf16[2,2,384]{2,1,0:T(2,128)(2,1)S(1)} %get-tuple-element.88), channel_id=1, source_target_pairs={{0,4},{4,8},{8,12},{1,5},{5,9},{9,13},{2,6},{6,10},{10,14},{3,7},{... | collective-permute-start | bytes 9224 | tf_op jit(solution)/shard_map/ppermute | solution.py:34
  15.4 1.3 collective-permute-start.1
  16.7 4.2 %collective-permute-done.1 = bf16[2,2,384]{2,1,0:T(2,128)(2,1)S(1)} collective-permute-done((bf16[2,2,384]{2,1,0:T(2,128)(2,1)S(1)}, bf16[2,2,384]{2,1,0:T(2,128)(2,1)S(1)}, u32[]{:S(2)}, u32[]{:S(2)}) %collective-permute-start.1) | collective-permute-done | bytes 3104 | tf_op jit(solution)/shard_map/ppermute | solution.py:36
  20.9 26.7 %all-gather.4.cloned.1.call-done = bf16[5,384,384]{2,1,0:T(8,128)(2,1)} async-done(((bf16[5,96,384]{2,1,0:T(8,128)(2,1)}), bf16[5,384,384]{2,1,0:T(8,128)(2,1)}) %all-gather.4.cloned.1.call-update) | async-done | bytes 1474576 | tf_op jit(solution)/shard_map/all_gather | solution.py:125
  47.6 1.3 fusion.39
  49.0 1.2 fusion.33
  50.9 1.1 fusion.32
  52.6 1.9 all-gather
  54.7 33.8 %all-gather.6.cloned.1.call-done = bf16[3,768,384]{2,1,0:T(8,128)(2,1)} async-done(((bf16[3,192,384]{2,1,0:T(8,128)(2,1)}), bf16[3,768,384]{2,1,0:T(8,128)(2,1)}) %all-gather.6.cloned.1.call-update) | async-done | bytes 1769488 | tf_op jit(solution)/shard_map/all_gather | solution.py:146
  88.5 2.0 fusion.8
  90.6 0.9 reshape.242
  91.5 3.3 %all-to-all-start = ((bf16[4,2,6144]{2,1,0:T(2,128)(2,1)}), bf16[4,2,6144]{2,1,0:T(2,128)(2,1)S(1)}, u32[]{:S(2)}, u32[]{:S(2)}) async-start(bf16[4,2,6144]{2,1,0:T(2,128)(2,1)} %reshape.242), calls=%async_computation | async-start | bytes 196608 | tf_op jit(solution)/shard_map/all_to_all | solution.py:174
  95.3 1.0 reshape_reshape.4
  96.3 4.3 %all-to-all-done = bf16[4,2,6144]{2,1,0:T(2,128)(2,1)S(1)} async-done(((bf16[4,2,6144]{2,1,0:T(2,128)(2,1)}), bf16[4,2,6144]{2,1,0:T(2,128)(2,1)S(1)}, u32[]{:S(2)}, u32[]{:S(2)}) %all-to-all-start) | async-done | bytes 98336 | tf_op jit(solution)/shard_map/all_to_all | solution.py:174
  100.6 3.4 %all-to-all-start.1 = ((bf16[4,2,12288]{2,1,0:T(2,128)(2,1)}), bf16[4,2,12288]{2,1,0:T(2,128)(2,1)S(1)}, u32[]{:S(2)}, u32[]{:S(2)}) async-start(bf16[4,2,12288]{2,1,0:T(2,128)(2,1)} %reshape_reshape.4), calls=%async_computation.1 | async-start | bytes 393216 | tf_op jit(solution)/shard_map/all_to_all | solution.py:175
  104.1 2.0 collective-permute-start.2
  106.2 1.9 collective-permute-start.4
  108.0 8.9 %collective-permute-done.2 = bf16[384,192]{1,0:T(8,128)(2,1)S(1)} collective-permute-done((bf16[384,192]{1,0:T(8,128)(2,1)S(1)}, bf16[384,192]{1,0:T(8,128)(2,1)S(1)}, u32[]{:S(2)}, u32[]{:S(2)}) %collective-permute-start.2) | collective-permute-done | bytes 147488 | tf_op jit(solution)/shard_map/ppermute | solution.py:19
  122.0 4.4 %all-to-all-start.2 = ((bf16[4,2,6144]{2,1,0:T(2,128)(2,1)}), bf16[4,2,6144]{2,1,0:T(2,128)(2,1)S(1)}, u32[]{:S(2)}, u32[]{:S(2)}) async-start(bf16[4,2,6144]{2,1,0:T(2,128)(2,1)} %copy.123), calls=%async_computation.2 | async-start | bytes 196608 | tf_op jit(solution)/shard_map/all_to_all | solution.py:192
  127.0 2.5 concatenate.36
  129.5 2.6 %all-to-all-done.2 = bf16[4,2,6144]{2,1,0:T(2,128)(2,1)S(1)} async-done(((bf16[4,2,6144]{2,1,0:T(2,128)(2,1)}), bf16[4,2,6144]{2,1,0:T(2,128)(2,1)S(1)}, u32[]{:S(2)}, u32[]{:S(2)}) %all-to-all-start.2) | async-done | bytes 98336 | tf_op jit(solution)/shard_map/all_to_all | solution.py:192
  132.4 0.8 reshape.245
  133.2 2.0 convolution_convert_fusion
  135.2 1.3 copy.151
  136.5 0.9 reshape.261
  137.4 1.3 dynamic_slice.25
  138.8 15.2 %all_gather.21 = bf16[384,768]{0,1:T(8,128)(2,1)S(1)} all-gather(bf16[384,192]{0,1:T(8,128)(2,1)S(1)} %copy-done.9), channel_id=1, replica_groups=mesh['group'=2,'seq'=4,'batch'=2,'mp'=2] {'seq'}, dimensions={1}, use_global_device_ids=true | all-gather | bytes 737280 | tf_op jit(solution)/shard_map/all_gather | solution.py:254
  154.7 0.8 squeeze.90
  156.3 1.0 reshape.262
  157.5 2.0 all_gather.20
  160.5 0.9 reduce.9
  162.1 3.3 %all-to-all-start.3 = ((bf16[4,2,3072]{2,1,0:T(2,128)(2,1)}), bf16[4,2,3072]{2,1,0:T(2,128)(2,1)S(1)}, u32[]{:S(2)}, u32[]{:S(2)}) async-start(bf16[4,2,3072]{2,1,0:T(2,128)(2,1)} %reshape.271), calls=%async_computation.3 | async-start | bytes 98304 | tf_op jit(solution)/shard_map/all_to_all | solution.py:262
  165.6 5.5 %all-to-all-done.3 = bf16[4,2,3072]{2,1,0:T(2,128)(2,1)S(1)} async-done(((bf16[4,2,3072]{2,1,0:T(2,128)(2,1)}), bf16[4,2,3072]{2,1,0:T(2,128)(2,1)S(1)}, u32[]{:S(2)}, u32[]{:S(2)}) %all-to-all-start.3) | async-done | bytes 49184 | tf_op jit(solution)/shard_map/all_to_all | solution.py:262
  172.8 0.9 reduce.11
  174.4 3.5 %all-to-all-start.4 = ((bf16[4,2,3072]{2,1,0:T(2,128)(2,1)}), bf16[4,2,3072]{2,1,0:T(2,128)(2,1)S(1)}, u32[]{:S(2)}, u32[]{:S(2)}) async-start(bf16[4,2,3072]{2,1,0:T(2,128)(2,1)} %reshape.275), calls=%async_computation.4 | async-start | bytes 98304 | tf_op jit(solution)/shard_map/all_to_all | solution.py:273
  178.2 1.2 reduce.10
  179.4 0.8 reshape.273
  180.2 3.2 %all-to-all-done.4 = bf16[4,2,3072]{2,1,0:T(2,128)(2,1)S(1)} async-done(((bf16[4,2,3072]{2,1,0:T(2,128)(2,1)}), bf16[4,2,3072]{2,1,0:T(2,128)(2,1)S(1)}, u32[]{:S(2)}, u32[]{:S(2)}) %all-to-all-start.4) | async-done | bytes 49184 | tf_op jit(solution)/shard_map/all_to_all | solution.py:273
  183.9 3.9 %all-to-all-start.5 = ((bf16[4,2,6144]{2,1,0:T(2,128)(2,1)}), bf16[4,2,6144]{2,1,0:T(2,128)(2,1)}, u32[]{:S(2)}, u32[]{:S(2)}) async-start(bf16[4,2,6144]{2,1,0:T(2,128)(2,1)} %reshape.273), calls=%async_computation.5 | async-start | bytes 196608 | tf_op jit(solution)/shard_map/all_to_all | solution.py:280
  187.9 1.0 reshape.276
  188.9 0.9 reduce.4
  189.8 0.9 convert_element_type.211
  191.4 1.6 convert_element_type.213
  193.0 0.8 all-to-all-done.5
  193.8 1.7 reshape.274
  195.4 1.5 reduce.5
  196.9 0.8 convert_element_type.216
  197.7 1.2 fusion.125
  200.4 0.9 copy.139
  202.0 1.5 fusion.17
  203.5 0.8 copy.153
  204.4 8.3 %reduce-scatter.9.cloned.1.call-done = bf16[384,64]{1,0:T(8,128)(2,1)} async-done(((bf16[768,64]{1,0:T(8,128)(2,1)}), bf16[384,64]{1,0:T(8,128)(2,1)}) %reduce-scatter.9.cloned.1.call-update) | async-done | bytes 49168
  212.7 1.0 copy.154
  213.7 1.0 fusion.107
  214.7 2.5 psum.14
  217.2 1.0 broadcast_multiply_fusion
  218.6 3.6 %collective-permute-start.6 = (bf16[2,384]{1,0:T(2,128)(2,1)S(1)}, bf16[2,384]{1,0:T(2,128)(2,1)S(1)}, u32[]{:S(2)}, u32[]{:S(2)}) collective-permute-start(bf16[2,384]{1,0:T(2,128)(2,1)S(1)} %get-tuple-element.93), channel_id=1, source_target_pairs={{0,4},{4,8},{8,12},{1,5},{5,9},{9,13},{2,6},{6,10},{10,14},{3,7},{... | collective-permute-start | bytes 4616 | tf_op jit(solution)/shard_map/ppermute | solution.py:34
  222.5 1.3 collective-permute-start.5
  224.3 3.7 %collective-permute-done.5 = bf16[2,384]{1,0:T(2,128)(2,1)S(1)} collective-permute-done((bf16[2,384]{1,0:T(2,128)(2,1)S(1)}, bf16[2,384]{1,0:T(2,128)(2,1)S(1)}, u32[]{:S(2)}, u32[]{:S(2)}) %collective-permute-start.5) | collective-permute-done | bytes 1568 | tf_op jit(solution)/shard_map/ppermute | solution.py:36
  228.5 0.9 fusion.18
  230.0 17.4 %all-reduce.2.cloned.1.call-done = bf16[128,384]{1,0:T(8,128)(2,1)} async-done(((bf16[128,384]{1,0:T(8,128)(2,1)}), bf16[128,384]{1,0:T(8,128)(2,1)}) %all-reduce.2.cloned.1.call-update) | async-done | bytes 98320 | tf_op jit(solution)/shard_map/psum | solution.py:334
  247.4 1.0 fusion.59
  248.4 1.7 fusion.61
  (148 shorter events, 22.2 us)
Async XLA Ops:
  7.2 13.7 %copy-start.4 = (bf16[1,128,384]{2,1,0:T(8,128)(2,1)S(1)}, bf16[1,128,384]{2,1,0:T(8,128)(2,1)}, u32[]{:S(2)}) copy-start(bf16[1,128,384]{2,1,0:T(8,128)(2,1)} %param.7) | copy-start | bytes 294916
  7.2 40.5 %all-gather.4.cloned.1.call-start = ((), (), s32[]{:S(2)}) async-start(), calls=%async_computation.8 | async-start | bytes 1843200 | tf_op jit(solution)/shard_map/all_gather | solution.py:125
  7.9 80.5 %all-gather.6.cloned.1.call-start = ((), (), s32[]{:S(2)}) async-start(), calls=%async_computation.9 | async-start | bytes 2211840 | tf_op jit(solution)/shard_map/all_gather | solution.py:146
  10.4 6.3 %collective-permute-start = (bf16[2,2,384]{2,1,0:T(2,128)(2,1)S(1)}, bf16[2,2,384]{2,1,0:T(2,128)(2,1)S(1)}, u32[]{:S(2)}, u32[]{:S(2)}) collective-permute-start(bf16[2,2,384]{2,1,0:T(2,128)(2,1)S(1)} %get-tuple-element.88), channel_id=1, source_target_pairs={{0,4},{4,8},{8,12},{1,5},{5,9},{9,13},{2,6},{6,10},{10,14},{3,7},{... | collective-permute-start | bytes 9224 | tf_op jit(solution)/shard_map/ppermute | solution.py:34
  15.4 5.5 %collective-permute-start.1 = (bf16[2,2,384]{2,1,0:T(2,128)(2,1)S(1)}, bf16[2,2,384]{2,1,0:T(2,128)(2,1)S(1)}, u32[]{:S(2)}, u32[]{:S(2)}) collective-permute-start(bf16[2,2,384]{2,1,0:T(2,128)(2,1)S(1)} %get-tuple-element.89), channel_id=1, source_target_pairs={{4,0},{8,4},{12,8},{5,1},{9,5},{13,9},{6,2},{10,6},{14,10},{7,3},{... | collective-permute-start | bytes 9224 | tf_op jit(solution)/shard_map/ppermute | solution.py:36
  47.6 2.6 %copy-start.1 = (bf16[5,384,384]{2,1,0:T(8,128)(2,1)S(1)}, bf16[5,384,384]{2,1,0:T(8,128)(2,1)}, u32[]{:S(2)}) copy-start(bf16[5,384,384]{2,1,0:T(8,128)(2,1)} %all-gather.4.cloned.1.call-done) | copy-start | bytes 4423684
  50.2 0.7 copy-start.19
  52.0 36.4 %copy-start.13 = (f32[768]{0:T(1024)S(1)}, f32[768]{0:T(1024)}, u32[]{:S(2)}) copy-start(f32[768]{0:T(1024)} %param.11) | copy-start | bytes 9220
  54.7 33.8 %copy-start.17 = (f32[2,64]{1,0:T(2,128)}, f32[2,64]{1,0:T(2,128)S(1)}, u32[]{:S(2)}) copy-start(f32[2,64]{1,0:T(2,128)S(1)} %add_rsqrt_fusion) | copy-start | bytes 1540
  90.6 13.4 %copy-start.9 = (bf16[384,192]{0,1:T(8,128)(2,1)S(1)}, bf16[384,192]{0,1:T(8,128)(2,1)}, u32[]{:S(2)}) copy-start(bf16[384,192]{0,1:T(8,128)(2,1)} %param.13) | copy-start | bytes 442372
  91.5 9.1 %all-to-all-start = ((bf16[4,2,6144]{2,1,0:T(2,128)(2,1)}), bf16[4,2,6144]{2,1,0:T(2,128)(2,1)S(1)}, u32[]{:S(2)}, u32[]{:S(2)}) async-start(bf16[4,2,6144]{2,1,0:T(2,128)(2,1)} %reshape.242), calls=%async_computation | async-start | bytes 196608 | tf_op jit(solution)/shard_map/all_to_all | solution.py:174
  100.6 17.7 %all-to-all-start.1 = ((bf16[4,2,12288]{2,1,0:T(2,128)(2,1)}), bf16[4,2,12288]{2,1,0:T(2,128)(2,1)S(1)}, u32[]{:S(2)}, u32[]{:S(2)}) async-start(bf16[4,2,12288]{2,1,0:T(2,128)(2,1)} %reshape_reshape.4), calls=%async_computation.1 | async-start | bytes 393216 | tf_op jit(solution)/shard_map/all_to_all | solution.py:175
  104.1 12.8 %collective-permute-start.2 = (bf16[384,192]{1,0:T(8,128)(2,1)S(1)}, bf16[384,192]{1,0:T(8,128)(2,1)S(1)}, u32[]{:S(2)}, u32[]{:S(2)}) collective-permute-start(bf16[384,192]{1,0:T(8,128)(2,1)S(1)} %copy.125), channel_id=1, source_target_pairs={{0,4},{4,8},{8,12},{12,0},{1,5},{5,9},{9,13},{13,1},{2,6},{6,10},{... | collective-permute-start | bytes 442376 | tf_op jit(solution)/shard_map/ppermute | solution.py:19
  106.2 20.2 %collective-permute-start.4 = (bf16[384,192]{1,0:T(8,128)(2,1)S(1)}, bf16[384,192]{1,0:T(8,128)(2,1)S(1)}, u32[]{:S(2)}, u32[]{:S(2)}) collective-permute-start(bf16[384,192]{1,0:T(8,128)(2,1)S(1)} %copy.125), channel_id=1, source_target_pairs={{0,12},{4,0},{8,4},{12,8},{1,13},{5,1},{9,5},{13,9},{2,14},{6,2},{... | collective-permute-start | bytes 442376 | tf_op jit(solution)/shard_map/ppermute | solution.py:21
  116.9 3.6 %copy-start.7 = (bf16[384,192]{1,0:T(8,128)(2,1)}, bf16[384,192]{1,0:T(8,128)(2,1)S(1)}, u32[]{:S(2)}) copy-start(bf16[384,192]{1,0:T(8,128)(2,1)S(1)} %collective-permute-done.2) | copy-start | bytes 442372
  116.9 10.1 %collective-permute-start.3 = (bf16[384,192]{1,0:T(8,128)(2,1)S(1)}, bf16[384,192]{1,0:T(8,128)(2,1)}, u32[]{:S(2)}, u32[]{:S(2)}) collective-permute-start(bf16[384,192]{1,0:T(8,128)(2,1)S(1)} %collective-permute-done.2), channel_id=1, source_target_pairs={{0,4},{4,8},{8,12},{12,0},{1,5},{5,9},{9,13},{13,1},{2,6},{6,10},{... | collective-permute-start | bytes 442376 | tf_op jit(solution)/shard_map/ppermute | solution.py:19
  119.1 0.6 copy-start.15
  120.0 6.4 %copy-start.10 = (bf16[256,96]{0,1:T(8,128)(2,1)}, bf16[256,96]{0,1:T(8,128)(2,1)S(1)}, u32[]{:S(2)}) copy-start(bf16[256,96]{0,1:T(8,128)(2,1)S(1)} %convolution_convert_fusion.3) | copy-start | bytes 147460
  122.0 10.2 %all-to-all-start.2 = ((bf16[4,2,6144]{2,1,0:T(2,128)(2,1)}), bf16[4,2,6144]{2,1,0:T(2,128)(2,1)S(1)}, u32[]{:S(2)}, u32[]{:S(2)}) async-start(bf16[4,2,6144]{2,1,0:T(2,128)(2,1)} %copy.123), calls=%async_computation.2 | async-start | bytes 196608 | tf_op jit(solution)/shard_map/all_to_all | solution.py:192
  126.3 29.9 %reduce-scatter.7.cloned.1.call-start = ((), (), s32[]{:S(2)}) async-start(), calls=%async_computation.11 | async-start | bytes 294912
  126.3 0.7 copy-start.8
  133.2 21.4 %copy-start.2 = (f32[2,128,384]{2,1,0:T(8,128)S(1)}, f32[2,128,384]{2,1,0:T(8,128)}, u32[]{:S(2)}) copy-start(f32[2,128,384]{2,1,0:T(8,128)} %get-tuple-element.95) | copy-start | bytes 1179652
  156.2 9.1 %copy-start.16 = (f32[256]{0:T(256)S(1)}, f32[256]{0:T(256)}, u32[]{:S(2)}) copy-start(f32[256]{0:T(256)} %copy-done.15) | copy-start | bytes 3076
  157.5 14.3 %copy-start.11 = (bf16[256,96]{0,1:T(8,128)(2,1)S(1)}, bf16[256,96]{0,1:T(8,128)(2,1)}, u32[]{:S(2)}) copy-start(bf16[256,96]{0,1:T(8,128)(2,1)} %copy-done.10) | copy-start | bytes 147460
  162.1 8.9 %all-to-all-start.3 = ((bf16[4,2,3072]{2,1,0:T(2,128)(2,1)}), bf16[4,2,3072]{2,1,0:T(2,128)(2,1)S(1)}, u32[]{:S(2)}, u32[]{:S(2)}) async-start(bf16[4,2,3072]{2,1,0:T(2,128)(2,1)} %reshape.271), calls=%async_computation.3 | async-start | bytes 98304 | tf_op jit(solution)/shard_map/all_to_all | solution.py:262
  171.8 16.1 %copy-start.18 = (f32[2,64]{1,0:T(2,128)S(1)}, f32[2,64]{1,0:T(2,128)}, u32[]{:S(2)}) copy-start(f32[2,64]{1,0:T(2,128)} %copy-done.17) | copy-start | bytes 1540
  174.4 8.9 %all-to-all-start.4 = ((bf16[4,2,3072]{2,1,0:T(2,128)(2,1)}), bf16[4,2,3072]{2,1,0:T(2,128)(2,1)S(1)}, u32[]{:S(2)}, u32[]{:S(2)}) async-start(bf16[4,2,3072]{2,1,0:T(2,128)(2,1)} %reshape.275), calls=%async_computation.4 | async-start | bytes 98304 | tf_op jit(solution)/shard_map/all_to_all | solution.py:273
  183.3 0.6 copy-start.12
  183.9 9.8 %all-to-all-start.5 = ((bf16[4,2,6144]{2,1,0:T(2,128)(2,1)}), bf16[4,2,6144]{2,1,0:T(2,128)(2,1)}, u32[]{:S(2)}, u32[]{:S(2)}) async-start(bf16[4,2,6144]{2,1,0:T(2,128)(2,1)} %reshape.273), calls=%async_computation.5 | async-start | bytes 196608 | tf_op jit(solution)/shard_map/all_to_all | solution.py:280
  187.9 14.2 %copy-start = (bf16[3,768,384]{2,1,0:T(8,128)(2,1)S(1)}, bf16[3,768,384]{2,1,0:T(8,128)(2,1)}, u32[]{:S(2)}) copy-start(bf16[3,768,384]{2,1,0:T(8,128)(2,1)} %all-gather.6.cloned.1.call-done) | copy-start | bytes 5308420
  187.9 24.8 %reduce-scatter.9.cloned.1.call-start = ((), (), s32[]{:S(2)}) async-start(), calls=%async_computation.12 | async-start | bytes 294912
  200.4 13.3 %copy-start.14 = (f32[384]{0:T(512)S(1)}, f32[384]{0:T(512)}, u32[]{:S(2)}) copy-start(f32[384]{0:T(512)} %dynamic_slice.25) | copy-start | bytes 4612
  203.5 14.9 %copy-start.3 = (f32[2,128,384]{2,1,0:T(8,128)S(1)}, f32[2,128,384]{2,1,0:T(8,128)}, u32[]{:S(2)}) copy-start(f32[2,128,384]{2,1,0:T(8,128)} %get-tuple-element.95) | copy-start | bytes 1179652
  203.5 18.7 %copy-start.6 = (f32[64,2,384]{2,1,0:T(2,128)S(1)}, f32[64,2,384]{2,1,0:T(2,128)}, u32[]{:S(2)}) copy-start(f32[64,2,384]{2,1,0:T(2,128)} %squeeze.90) | copy-start | bytes 589828
  204.4 43.0 %all-reduce.2.cloned.1.call-start = ((), (), s32[]{:S(2)}) async-start(), calls=%async_computation.10 | async-start | bytes 196608 | tf_op jit(solution)/shard_map/psum | solution.py:334
  218.6 5.5 %collective-permute-start.6 = (bf16[2,384]{1,0:T(2,128)(2,1)S(1)}, bf16[2,384]{1,0:T(2,128)(2,1)S(1)}, u32[]{:S(2)}, u32[]{:S(2)}) collective-permute-start(bf16[2,384]{1,0:T(2,128)(2,1)S(1)} %get-tuple-element.93), channel_id=1, source_target_pairs={{0,4},{4,8},{8,12},{1,5},{5,9},{9,13},{2,6},{6,10},{10,14},{3,7},{... | collective-permute-start | bytes 4616 | tf_op jit(solution)/shard_map/ppermute | solution.py:34
  222.5 5.5 %collective-permute-start.5 = (bf16[2,384]{1,0:T(2,128)(2,1)S(1)}, bf16[2,384]{1,0:T(2,128)(2,1)S(1)}, u32[]{:S(2)}, u32[]{:S(2)}) collective-permute-start(bf16[2,384]{1,0:T(2,128)(2,1)S(1)} %get-tuple-element.92), channel_id=1, source_target_pairs={{4,0},{8,4},{12,8},{5,1},{9,5},{13,9},{6,2},{10,6},{14,10},{7,3},{... | collective-permute-start | bytes 4616 | tf_op jit(solution)/shard_map/ppermute | solution.py:36
  224.3 24.1 %copy-start.5 = (f32[1,128,384]{2,1,0:T(8,128)S(1)}, f32[1,128,384]{2,1,0:T(8,128)}, u32[]{:S(2)}) copy-start(f32[1,128,384]{2,1,0:T(8,128)} %param.8) | copy-start | bytes 589828
Sparse Core Ops, SparseCore 0:
  9.6 38.0 all-gather.3
  49.2 39.1 all-gather.5
  137.5 6.3 reduce-scatter.6
  204.5 8.1 reduce-scatter.8
  229.5 17.8 all-reduce.1
